TPU v7x, 256 devices: a whole 4x4x8 slice. The times are simulated.
256 devices in a mesh: dp: 32 (over x, y, core), tensor: 8 (over z).
Axes of the slice: x: 4, y: 4, z: 8, core: 2. Of those that a mesh axis runs over, the one named last changes fastest.
Arguments:
- hidden_states: bfloat16 [24576, 4096], P('dp', 'tensor')
- neighbour_ids: int32 [384, 2], P('dp'), may hold values from 0 to 511, as said below
- database: bfloat16 [512, 128, 896], P('dp')
- w_up: bfloat16 [896, 3584], P(None, 'tensor'), may hold values from -0.1875 to 0.1875
- w_down: bfloat16 [3584, 896], P('tensor'), may hold values from -0.09375 to 0.09375
- w_query: bfloat16 [4096, 4096], P(None, 'tensor'), may hold values from -0.09375 to 0.09375
- w_key: bfloat16 [896, 4096], P(None, 'tensor'), may hold values from -0.1875 to 0.1875
- w_value: bfloat16 [896, 4096], P(None, 'tensor'), may hold values from -0.1875 to 0.1875
Outputs:
- attended: bfloat16 [24576, 4096], P('dp', 'tensor')
Inputs may be any that keep to these rules, and one draw needn't show every extreme that they name: `neighbour_ids`: block ids are grouped by owner: index s of dp holds blocks s * 16 to (s + 1) * 16 - 1. Among the 24 ids of one sequence, no owner's blocks are named more than 2 times; one owner, the same for every sequence, is named exactly 2 times by each.
All inputs are finite; a program needn't handle non-finite values.
Results may differ from a plain program's by a relative error of at most 0.02.
Values may be sent and summed in bfloat16 or wider, within the bound.
No kernel may reach another device: no remote copies, remote signals or barrier semaphores. Data moves between devices by JAX's collectives and lax.ppermute only.
A program may use at most 128 MiB of HBM per device.

v0:
```python
import math
import jax
import jax.numpy as jnp
from jax import lax
from jax.sharding import PartitionSpec as P

HD = 128
SPAN = 64
KN = 2
NTOK = 128
EPSILON = 1e-06
LOGIT_SCALE = 3.0


def head_norm(projected):
    shaped = projected.reshape(projected.shape[0], -1, HD)
    scaled = shaped * lax.rsqrt(jnp.mean(shaped * shaped, axis=-1, keepdims=True) + EPSILON)
    return scaled.astype(jnp.bfloat16)


def attend(queries, keys, values):
    heads_here = queries.shape[0]
    seq_rows = queries.shape[1] + SPAN - 1
    span_count = seq_rows // SPAN
    shifted = jnp.concatenate(
        [queries, jnp.zeros((heads_here, SPAN - 1, HD), jnp.bfloat16)], axis=1
    )
    windows = shifted.reshape(heads_here, span_count, SPAN, HD)
    key_blocks = keys.reshape(heads_here, span_count, KN * NTOK, HD)
    value_blocks = values.reshape(heads_here, span_count, KN * NTOK, HD)
    scores = jnp.einsum("hcqd,hckd->hcqk", windows, key_blocks, preferred_element_type=jnp.float32)
    scores = scores * (LOGIT_SCALE / math.sqrt(HD))
    expo = jnp.exp(scores)
    weights = (expo / jnp.sum(expo, axis=-1, keepdims=True)).astype(jnp.bfloat16)
    mixed = jnp.einsum("hcqk,hckd->cqhd", weights, value_blocks, preferred_element_type=jnp.float32)
    mixed = mixed.astype(jnp.bfloat16).reshape(seq_rows, heads_here * HD)
    leading = jnp.zeros((SPAN - 1, heads_here * HD), jnp.bfloat16)
    return jnp.concatenate([leading, mixed[: seq_rows - SPAN + 1]], axis=0)


def head_norm_major(projected):
    scaled = projected * lax.rsqrt(
        jnp.mean(projected * projected, axis=-1, keepdims=True) + EPSILON
    )
    return scaled.astype(jnp.bfloat16)


def ring_hops(states, n):
    to_right = [(i, (i + 1) % n) for i in range(n)]
    to_left = [(i, (i - 1) % n) for i in range(n)]
    going_right = states
    going_left = states
    right_hops = n // 2
    left_hops = n - 1 - right_hops
    steps = []
    for hop in range(1, right_hops + 1):
        step = {}
        going_right = lax.ppermute(going_right, "tensor", to_right)
        step[(n - hop) % n] = going_right
        if hop <= left_hops:
            going_left = lax.ppermute(going_left, "tensor", to_left)
            step[hop] = going_left
        steps.append(step)
    return steps


def ring_query(got, w_query, n):
    width = got[0].shape[1]
    me = lax.axis_index("tensor")
    total = None
    for offset in range(n):
        rows = lax.dynamic_slice_in_dim(w_query, (me + offset) % n * width, width, 0)
        term = jnp.dot(got[offset], rows, preferred_element_type=jnp.float32)
        total = term if total is None else total + term
    return total


def shards(hidden_states, neighbour_ids, database, w_up, w_down, w_query, w_key, w_value):
    dp_count = lax.axis_size("dp")
    tensor_count = lax.axis_size("tensor")
    shard_blocks = database.shape[0]
    block_tokens = database.shape[1]
    enc_width = database.shape[2]
    flat_ids = neighbour_ids.reshape(-1)
    request_count = flat_ids.shape[0]
    capacity = max(2, (request_count + dp_count - 1) // dp_count + 1)
    owners = flat_ids // shard_blocks
    local_rows = flat_ids % shard_blocks
    owner_match = (owners[:, None] == jnp.arange(dp_count, dtype=jnp.int32)[None, :]).astype(
        jnp.int32
    )
    positions = jnp.arange(request_count, dtype=jnp.int32)
    earlier = (positions[:, None] > positions[None, :]).astype(jnp.int32)
    ranks = jnp.sum(jnp.dot(earlier, owner_match) * owner_match, axis=1)
    slots = owners * capacity + ranks
    slot_match = slots[None, :] == jnp.arange(dp_count * capacity, dtype=jnp.int32)[:, None]
    requests = jnp.sum(jnp.where(slot_match, local_rows[None, :], 0), axis=1)
    requests = requests.reshape(dp_count, capacity)
    raw_float = database.astype(jnp.float32)
    normed = (
        raw_float * lax.rsqrt(jnp.mean(raw_float * raw_float, axis=-1, keepdims=True) + EPSILON)
    ).astype(jnp.bfloat16)
    inner = jnp.einsum("bte,ef->btf", normed, w_up, preferred_element_type=jnp.float32)
    active = jax.nn.gelu(inner).astype(jnp.bfloat16)
    partial = jnp.einsum("btf,fe->bte", active, w_down, preferred_element_type=jnp.float32)
    rows_here = block_tokens // tensor_count
    states = hidden_states[SPAN - 1 :]
    head_rows = 3 * SPAN
    head_got = {0: states[:head_rows]}
    for step in ring_hops(states[:head_rows], tensor_count):
        head_got.update(step)
    summed = lax.psum_scatter(
        partial.astype(jnp.bfloat16), "tensor", scatter_dimension=1, tiled=True
    )
    states_rest, summed, head_got = lax.optimization_barrier((states[head_rows:], summed, head_got))
    summed = summed.astype(jnp.float32)
    raw_own = lax.dynamic_slice_in_dim(
        raw_float, lax.axis_index("tensor") * rows_here, rows_here, 1
    )
    encoded_own = (raw_own + summed).astype(jnp.bfloat16)
    asked = lax.all_to_all(requests, "dp", split_axis=0, concat_axis=0, tiled=True)
    replies = lax.all_to_all(encoded_own[asked], "dp", split_axis=0, concat_axis=0, tiled=True)
    mine = replies.reshape(dp_count * capacity, rows_here, enc_width)[slots]
    encoded = lax.all_gather(mine, "tensor", axis=1, tiled=True)
    heads_here = w_query.shape[1] // HD
    states_rest = lax.all_gather(states_rest, "tensor", axis=1, tiled=True)
    projected = jnp.concatenate(
        [
            ring_query(head_got, w_query, tensor_count),
            jnp.dot(states_rest, w_query, preferred_element_type=jnp.float32),
        ],
        axis=0,
    )
    queries = head_norm_major(projected.reshape(projected.shape[0], heads_here, HD))
    queries = jnp.transpose(queries, (1, 0, 2))
    flat_encoded = encoded.reshape(-1, enc_width)
    keys = head_norm_major(
        jnp.einsum(
            "ke,ehd->hkd",
            flat_encoded,
            w_key.reshape(enc_width, heads_here, HD),
            preferred_element_type=jnp.float32,
        )
    )
    values = jnp.einsum(
        "ke,ehd->hkd",
        flat_encoded,
        w_value.reshape(enc_width, heads_here, HD),
        preferred_element_type=jnp.float32,
    ).astype(jnp.bfloat16)
    return attend(queries, keys, values)


def solution(mesh):
    in_specs = (
        P("dp", "tensor"),
        P("dp", None),
        P("dp", None, None),
        P(None, "tensor"),
        P("tensor", None),
        P(None, "tensor"),
        P(None, "tensor"),
        P(None, "tensor"),
    )
    out_specs = P("dp", "tensor")
    return jax.shard_map(shards, mesh=mesh, in_specs=in_specs, out_specs=out_specs, check_vma=False)
```

profile of v0, /device:TPU:1, one launch (start us, length us, event | category | flops | bytes accessed | tf_op | source)
XLA Modules:
  0.0 229.0 jit_solution(14006398751083424595)
XLA Ops:
  6.5 3.0 %multiply_reduce_fusion = f32[16,128]{1,0:T(8,128)S(1)} fusion(bf16[16,128,896]{2,1,0:T(8,128)(2,1)} %param.10), kind=kLoop, calls=%fused_computation.3 | loop fusion | flops 5502976 | bytes 3678208 | tf_op jit(solution)/shard_map/reduce_sum | solution.py:101
  9.6 7.7 %convolution_convert_fusion.1 = bf16[16,128,896]{2,1,0:T(8,128)(2,1)} fusion(f32[16,128]{1,0:T(8,128)S(1)} %add_rsqrt_fusion.2, bf16[16,128,896]{2,1,0:T(8,128)(2,1)} %param.10, bf16[448,896]{1,0:T(8,128)(2,1)S(1)} %copy-done.14, bf16[896,448]{0,1:T(8,128)(2,1)S(1)} %copy-done.15), kind=kOutput, calls=%fused_computation.26 | convolution fusion | flops 3303931904 | bytes 8953856 | tf_op jit(solution)/shard_map/btf,fe->bte/dot_general | solution.py:105
  18.4 2.5 %collective-permute-start.3 = (bf16[192,512]{1,0:T(8,128)(2,1)S(1)}, bf16[192,512]{1,0:T(8,128)(2,1)S(1)}, u32[]{:S(2)}, u32[]{:S(2)}) collective-permute-start(bf16[192,512]{1,0:T(8,128)(2,1)S(1)} %slice.14), channel_id=1, source_target_pairs={{0,1},{1,2},{2,3},{3,4},{4,5},{5,6},{6,7},{7,0},{8,9},{9,10},{10,1... | collective-permute-start | bytes 589832 | tf_op jit(solution)/shard_map/ppermute | solution.py:58
  21.0 4.0 %collective-permute-start = (bf16[192,512]{1,0:T(8,128)(2,1)S(1)}, bf16[192,512]{1,0:T(8,128)(2,1)S(1)}, u32[]{:S(2)}, u32[]{:S(2)}) collective-permute-start(bf16[192,512]{1,0:T(8,128)(2,1)S(1)} %slice.14), channel_id=1, source_target_pairs={{0,7},{1,0},{2,1},{3,2},{4,3},{5,4},{6,5},{7,6},{8,15},{9,8},{10,9... | collective-permute-start | bytes 589832 | tf_op jit(solution)/shard_map/ppermute | solution.py:61
  25.0 4.5 %collective-permute-done.3 = bf16[192,512]{1,0:T(8,128)(2,1)S(1)} collective-permute-done((bf16[192,512]{1,0:T(8,128)(2,1)S(1)}, bf16[192,512]{1,0:T(8,128)(2,1)S(1)}, u32[]{:S(2)}, u32[]{:S(2)}) %collective-permute-start.3) | collective-permute-done | bytes 196640 | tf_op jit(solution)/shard_map/ppermute | solution.py:58
  29.5 2.7 %collective-permute-start.1 = (bf16[192,512]{1,0:T(8,128)(2,1)S(1)}, bf16[192,512]{1,0:T(8,128)(2,1)S(1)}, u32[]{:S(2)}, u32[]{:S(2)}) collective-permute-start(bf16[192,512]{1,0:T(8,128)(2,1)S(1)} %collective-permute-done), channel_id=1, source_target_pairs={{0,7},{1,0},{2,1},{3,2},{4,3},{5,4},{6,5},{7,6},{8,15},{9,8},{10,9... | collective-permute-start | bytes 589832 | tf_op jit(solution)/shard_map/ppermute | solution.py:61
  32.2 3.7 %collective-permute-done.4 = bf16[192,512]{1,0:T(8,128)(2,1)S(1)} collective-permute-done((bf16[192,512]{1,0:T(8,128)(2,1)S(1)}, bf16[192,512]{1,0:T(8,128)(2,1)S(1)}, u32[]{:S(2)}, u32[]{:S(2)}) %collective-permute-start.4) | collective-permute-done | bytes 196640 | tf_op jit(solution)/shard_map/ppermute | solution.py:58
  35.9 4.0 %collective-permute-done.1 = bf16[192,512]{1,0:T(8,128)(2,1)S(1)} collective-permute-done((bf16[192,512]{1,0:T(8,128)(2,1)S(1)}, bf16[192,512]{1,0:T(8,128)(2,1)S(1)}, u32[]{:S(2)}, u32[]{:S(2)}) %collective-permute-start.1) | collective-permute-done | bytes 196640 | tf_op jit(solution)/shard_map/ppermute | solution.py:61
  39.9 3.5 %collective-permute-start.2 = (bf16[192,512]{1,0:T(8,128)(2,1)S(1)}, bf16[192,512]{1,0:T(8,128)(2,1)S(1)}, u32[]{:S(2)}, u32[]{:S(2)}) collective-permute-start(bf16[192,512]{1,0:T(8,128)(2,1)S(1)} %collective-permute-done.1), channel_id=1, source_target_pairs={{0,7},{1,0},{2,1},{3,2},{4,3},{5,4},{6,5},{7,6},{8,15},{9,8},{10,9... | collective-permute-start | bytes 589832 | tf_op jit(solution)/shard_map/ppermute | solution.py:61
  43.4 3.4 %collective-permute-done.5 = bf16[192,512]{1,0:T(8,128)(2,1)S(1)} collective-permute-done((bf16[192,512]{1,0:T(8,128)(2,1)S(1)}, bf16[192,512]{1,0:T(8,128)(2,1)S(1)}, u32[]{:S(2)}, u32[]{:S(2)}) %collective-permute-start.5) | collective-permute-done | bytes 196640 | tf_op jit(solution)/shard_map/ppermute | solution.py:58
  47.7 3.8 %collective-permute-done.2 = bf16[192,512]{1,0:T(8,128)(2,1)S(1)} collective-permute-done((bf16[192,512]{1,0:T(8,128)(2,1)S(1)}, bf16[192,512]{1,0:T(8,128)(2,1)S(1)}, u32[]{:S(2)}, u32[]{:S(2)}) %collective-permute-start.2) | collective-permute-done | bytes 196640 | tf_op jit(solution)/shard_map/ppermute | solution.py:61
  51.5 6.2 %collective-permute-done.6 = bf16[192,512]{1,0:T(8,128)(2,1)S(1)} collective-permute-done((bf16[192,512]{1,0:T(8,128)(2,1)S(1)}, bf16[192,512]{1,0:T(8,128)(2,1)S(1)}, u32[]{:S(2)}, u32[]{:S(2)}) %collective-permute-start.6) | collective-permute-done | bytes 196640 | tf_op jit(solution)/shard_map/ppermute | solution.py:58
  57.7 23.8 %reduce-scatter.2.cloned.1.call-done = bf16[16,16,896]{2,1,0:T(8,128)(2,1)} async-done(((bf16[16,128,896]{2,1,0:T(8,128)(2,1)}), bf16[16,16,896]{2,1,0:T(8,128)(2,1)}) %reduce-scatter.2.cloned.1.call-update) | async-done | bytes 458768 | tf_op jit(solution)/shard_map/reduce_scatter | solution.py:112
  82.8 7.6 %all-to-all-start = ((s32[32,1,2]{2,1,0:T(1,128)}), s32[32,1,2]{2,1,0:T(1,128)S(1)}, u32[]{:S(2)}, u32[]{:S(2)}) async-start(s32[32,1,2]{2,1,0:T(1,128)} %bitcast.2), calls=%async_computation.1 | async-start | bytes 32768 | tf_op jit(solution)/shard_map/all_to_all | solution.py:121
  90.5 5.8 %convert_element_type.41 = f32[16,128,896]{2,1,0:T(8,128)} convert(bf16[16,128,896]{2,1,0:T(8,128)(2,1)} %param.10) | non-fusion elementwise | flops 1835008 | bytes 11010048 | tf_op jit(solution)/shard_map/convert_element_type | solution.py:99
  97.7 1.3 add_convert_fusion
  98.9 2.0 gather_fusion
  100.9 6.4 %all-to-all-start.1 = ((bf16[32,2,16,896]{3,2,1,0:T(8,128)(2,1)}), bf16[32,2,16,896]{3,2,1,0:T(8,128)(2,1)S(1)}, u32[]{:S(2)}, u32[]{:S(2)}) async-start(bf16[32,2,16,896]{3,2,1,0:T(8,128)(2,1)} %bitcast.4), calls=%async_computation.2 | async-start | bytes 3670016 | tf_op jit(solution)/shard_map/all_to_all | solution.py:122
  107.7 25.2 %all-to-all-done.1 = bf16[32,2,16,896]{3,2,1,0:T(8,128)(2,1)S(1)} async-done(((bf16[32,2,16,896]{3,2,1,0:T(8,128)(2,1)}), bf16[32,2,16,896]{3,2,1,0:T(8,128)(2,1)S(1)}, u32[]{:S(2)}, u32[]{:S(2)}) %all-to-all-start.1) | async-done | bytes 1835040 | tf_op jit(solution)/shard_map/all_to_all | solution.py:122
  132.8 1.5 gather_fusion.1
  134.5 1.5 fusion.48
  136.0 1.4 fusion.50
  137.4 1.4 fusion.52
  138.8 1.3 fusion.54
  141.3 5.8 %fusion.77 = f32[513,512]{1,0:T(8,128)S(1)} fusion(bf16[513,4096]{1,0:T(8,128)(2,1)} %all-gather.4.cloned.1.call-done, bf16[4096,512]{1,0:T(8,128)(2,1)} %param.13), kind=kOutput, calls=%fused_computation.107 | convolution fusion | flops 2151677952 | bytes 9447424 | tf_op jit(solution)/shard_map/dot_general | solution.py:130
  148.5 1.7 reshape.246
  151.1 1.7 fusion.47
  152.9 52.7 %all-gather.6.cloned.1.call-done = bf16[24,128,896]{2,1,0:T(8,128)(2,1)} async-done(((bf16[24,16,896]{2,1,0:T(8,128)(2,1)}), bf16[24,128,896]{2,1,0:T(8,128)(2,1)}) %all-gather.6.cloned.1.call-update) | async-done | bytes 5505040 | tf_op jit(solution)/shard_map/all_gather | solution.py:124
  205.7 6.9 %fusion = (f32[4,3072]{1,0:T(4,128)S(1)}, f32[3072,4,128]{2,0,1:T(8,128)S(1)}) fusion(bf16[3072,896,1]{1,0,2:T(8,128)(2,1)} %bitcast.79, bf16[896,512]{1,0:T(8,128)(2,1)S(1)} %copy-done), kind=kOutput, calls=%fused_computation.6 | convolution fusion | flops 2821705728 | bytes 12763136 | tf_op jit(solution)/shard_map/ke,ehd->hkd/dot_general | solution.py:138
  212.6 3.6 %convolution_convert_fusion = bf16[3072,4,128]{2,0,1:T(8,128)(2,1)S(1)} fusion(bf16[3072,896,1]{1,0,2:T(8,128)(2,1)S(1)} %bitcast.80, bf16[896,512]{1,0:T(8,128)(2,1)S(1)} %copy-done.13), kind=kOutput, calls=%fused_computation.9 | convolution fusion | flops 2820145152 | bytes 9568256 | tf_op jit(solution)/shard_map/ke,ehd->hkd/dot_general | solution.py:145
  216.2 1.9 fusion.1
  218.2 1.3 fusion.15
  (77 shorter events, 11.6 us)
Async XLA Ops:
  6.5 199.1 %copy-start = (bf16[896,512]{1,0:T(8,128)(2,1)S(1)}, bf16[896,512]{1,0:T(8,128)(2,1)}, u32[]{:S(2)}) copy-start(bf16[896,512]{1,0:T(8,128)(2,1)} %param.14) | copy-start | bytes 2752516
  6.5 3.0 %copy-start.15 = (bf16[896,448]{0,1:T(8,128)(2,1)S(1)}, bf16[896,448]{0,1:T(8,128)(2,1)}, u32[]{:S(2)}) copy-start(bf16[896,448]{0,1:T(8,128)(2,1)} %param.11) | copy-start | bytes 2408452
  6.5 3.0 %copy-start.14 = (bf16[448,896]{1,0:T(8,128)(2,1)S(1)}, bf16[448,896]{1,0:T(8,128)(2,1)}, u32[]{:S(2)}) copy-start(bf16[448,896]{1,0:T(8,128)(2,1)} %param.12) | copy-start | bytes 2408452
  6.5 74.9 %reduce-scatter.2.cloned.1.call-start = ((), (), s32[]{:S(2)}) async-start(), calls=%async_computation.3 | async-start | bytes 4128768 | tf_op jit(solution)/shard_map/reduce_scatter | solution.py:112
  17.3 1.1 copy-start.3
  17.3 64.3 %copy-start.11 = (s32[12,2]{0,1:T(2,128)S(1)}, s32[12,2]{0,1:T(2,128)}, u32[]{:S(2)}) copy-start(s32[12,2]{0,1:T(2,128)} %param.9) | copy-start | bytes 292
  17.3 124.1 %all-gather.4.cloned.1.call-start = ((), (), s32[]{:S(2)}) async-start(), calls=%async_computation.4 | async-start | bytes 4792320 | tf_op jit(solution)/shard_map/all_gather | solution.py:126
  18.4 11.1 %collective-permute-start.3 = (bf16[192,512]{1,0:T(8,128)(2,1)S(1)}, bf16[192,512]{1,0:T(8,128)(2,1)S(1)}, u32[]{:S(2)}, u32[]{:S(2)}) collective-permute-start(bf16[192,512]{1,0:T(8,128)(2,1)S(1)} %slice.14), channel_id=1, source_target_pairs={{0,1},{1,2},{2,3},{3,4},{4,5},{5,6},{6,7},{7,0},{8,9},{9,10},{10,1... | collective-permute-start | bytes 589832 | tf_op jit(solution)/shard_map/ppermute | solution.py:58
  21.0 8.6 %collective-permute-start = (bf16[192,512]{1,0:T(8,128)(2,1)S(1)}, bf16[192,512]{1,0:T(8,128)(2,1)S(1)}, u32[]{:S(2)}, u32[]{:S(2)}) collective-permute-start(bf16[192,512]{1,0:T(8,128)(2,1)S(1)} %slice.14), channel_id=1, source_target_pairs={{0,7},{1,0},{2,1},{3,2},{4,3},{5,4},{6,5},{7,6},{8,15},{9,8},{10,9... | collective-permute-start | bytes 589832 | tf_op jit(solution)/shard_map/ppermute | solution.py:61
  29.5 6.4 %collective-permute-start.4 = (bf16[192,512]{1,0:T(8,128)(2,1)S(1)}, bf16[192,512]{1,0:T(8,128)(2,1)S(1)}, u32[]{:S(2)}, u32[]{:S(2)}) collective-permute-start(bf16[192,512]{1,0:T(8,128)(2,1)S(1)} %collective-permute-done.3), channel_id=1, source_target_pairs={{0,1},{1,2},{2,3},{3,4},{4,5},{5,6},{6,7},{7,0},{8,9},{9,10},{10,1... | collective-permute-start | bytes 589832 | tf_op jit(solution)/shard_map/ppermute | solution.py:58
  29.5 10.4 %collective-permute-start.1 = (bf16[192,512]{1,0:T(8,128)(2,1)S(1)}, bf16[192,512]{1,0:T(8,128)(2,1)S(1)}, u32[]{:S(2)}, u32[]{:S(2)}) collective-permute-start(bf16[192,512]{1,0:T(8,128)(2,1)S(1)} %collective-permute-done), channel_id=1, source_target_pairs={{0,7},{1,0},{2,1},{3,2},{4,3},{5,4},{6,5},{7,6},{8,15},{9,8},{10,9... | collective-permute-start | bytes 589832 | tf_op jit(solution)/shard_map/ppermute | solution.py:61
  35.9 54.5 %copy-start.5 = (bf16[192,512]{1,0:T(8,128)(2,1)}, bf16[192,512]{1,0:T(8,128)(2,1)S(1)}, u32[]{:S(2)}) copy-start(bf16[192,512]{1,0:T(8,128)(2,1)S(1)} %collective-permute-done.4) | copy-start | bytes 589828
  35.9 10.8 %collective-permute-start.5 = (bf16[192,512]{1,0:T(8,128)(2,1)S(1)}, bf16[192,512]{1,0:T(8,128)(2,1)S(1)}, u32[]{:S(2)}, u32[]{:S(2)}) collective-permute-start(bf16[192,512]{1,0:T(8,128)(2,1)S(1)} %collective-permute-done.4), channel_id=1, source_target_pairs={{0,1},{1,2},{2,3},{3,4},{4,5},{5,6},{6,7},{7,0},{8,9},{9,10},{10,1... | collective-permute-start | bytes 589832 | tf_op jit(solution)/shard_map/ppermute | solution.py:58
  39.9 11.6 %collective-permute-start.2 = (bf16[192,512]{1,0:T(8,128)(2,1)S(1)}, bf16[192,512]{1,0:T(8,128)(2,1)S(1)}, u32[]{:S(2)}, u32[]{:S(2)}) collective-permute-start(bf16[192,512]{1,0:T(8,128)(2,1)S(1)} %collective-permute-done.1), channel_id=1, source_target_pairs={{0,7},{1,0},{2,1},{3,2},{4,3},{5,4},{6,5},{7,6},{8,15},{9,8},{10,9... | collective-permute-start | bytes 589832 | tf_op jit(solution)/shard_map/ppermute | solution.py:61
  46.8 49.5 %copy-start.6 = (bf16[192,512]{1,0:T(8,128)(2,1)}, bf16[192,512]{1,0:T(8,128)(2,1)S(1)}, u32[]{:S(2)}) copy-start(bf16[192,512]{1,0:T(8,128)(2,1)S(1)} %collective-permute-done.5) | copy-start | bytes 589828
  46.8 10.9 %collective-permute-start.6 = (bf16[192,512]{1,0:T(8,128)(2,1)S(1)}, bf16[192,512]{1,0:T(8,128)(2,1)S(1)}, u32[]{:S(2)}, u32[]{:S(2)}) collective-permute-start(bf16[192,512]{1,0:T(8,128)(2,1)S(1)} %collective-permute-done.5), channel_id=1, source_target_pairs={{0,1},{1,2},{2,3},{3,4},{4,5},{5,6},{6,7},{7,0},{8,9},{9,10},{10,1... | collective-permute-start | bytes 589832 | tf_op jit(solution)/shard_map/ppermute | solution.py:58
  51.5 44.8 %copy-start.7 = (bf16[192,512]{1,0:T(8,128)(2,1)}, bf16[192,512]{1,0:T(8,128)(2,1)S(1)}, u32[]{:S(2)}) copy-start(bf16[192,512]{1,0:T(8,128)(2,1)S(1)} %collective-permute-done.2) | copy-start | bytes 589828
  57.7 38.7 %copy-start.9 = (bf16[192,512]{1,0:T(8,128)(2,1)}, bf16[192,512]{1,0:T(8,128)(2,1)S(1)}, u32[]{:S(2)}) copy-start(bf16[192,512]{1,0:T(8,128)(2,1)S(1)} %collective-permute-done.6) | copy-start | bytes 589828
  82.8 14.5 %all-to-all-start = ((s32[32,1,2]{2,1,0:T(1,128)}), s32[32,1,2]{2,1,0:T(1,128)S(1)}, u32[]{:S(2)}, u32[]{:S(2)}) async-start(s32[32,1,2]{2,1,0:T(1,128)} %bitcast.2), calls=%async_computation.1 | async-start | bytes 32768 | tf_op jit(solution)/shard_map/all_to_all | solution.py:121
  90.5 7.2 %copy-start.4 = (bf16[16,16,896]{2,1,0:T(8,128)(2,1)S(1)}, bf16[16,16,896]{2,1,0:T(8,128)(2,1)}, u32[]{:S(2)}) copy-start(bf16[16,16,896]{2,1,0:T(8,128)(2,1)} %reduce-scatter.2.cloned.1.call-done) | copy-start | bytes 1376260
  100.9 31.9 %all-to-all-start.1 = ((bf16[32,2,16,896]{3,2,1,0:T(8,128)(2,1)}), bf16[32,2,16,896]{3,2,1,0:T(8,128)(2,1)S(1)}, u32[]{:S(2)}, u32[]{:S(2)}) async-start(bf16[32,2,16,896]{3,2,1,0:T(8,128)(2,1)} %bitcast.4), calls=%async_computation.2 | async-start | bytes 3670016 | tf_op jit(solution)/shard_map/all_to_all | solution.py:122
  107.3 98.3 %all-gather.6.cloned.1.call-start = ((), (), s32[]{:S(2)}) async-start(), calls=%async_computation.5 | async-start | bytes 6193152 | tf_op jit(solution)/shard_map/all_gather | solution.py:124
  134.3 4.5 %copy-start.10 = (bf16[192,512]{1,0:T(8,128)(2,1)S(1)}, bf16[192,512]{1,0:T(8,128)(2,1)}, u32[]{:S(2)}) copy-start(bf16[192,512]{1,0:T(8,128)(2,1)} %copy-done.9) | copy-start | bytes 589828
  134.3 5.8 %copy-start.8 = (bf16[192,512]{1,0:T(8,128)(2,1)S(1)}, bf16[192,512]{1,0:T(8,128)(2,1)}, u32[]{:S(2)}) copy-start(bf16[192,512]{1,0:T(8,128)(2,1)} %copy-done.7) | copy-start | bytes 589828
  134.5 5.7 %copy-start.2 = (bf16[4096,512]{1,0:T(8,128)(2,1)S(1)}, bf16[4096,512]{1,0:T(8,128)(2,1)}, u32[]{:S(2)}) copy-start(bf16[4096,512]{1,0:T(8,128)(2,1)} %param.13) | copy-start | bytes 12582916
  205.7 6.9 %copy-start.12 = (bf16[24,128,896]{2,1,0:T(8,128)(2,1)S(1)}, bf16[24,128,896]{2,1,0:T(8,128)(2,1)}, u32[]{:S(2)}) copy-start(bf16[24,128,896]{2,1,0:T(8,128)(2,1)} %all-gather.6.cloned.1.call-done) | copy-start | bytes 16515076
  205.7 6.9 %copy-start.13 = (bf16[896,512]{1,0:T(8,128)(2,1)S(1)}, bf16[896,512]{1,0:T(8,128)(2,1)}, u32[]{:S(2)}) copy-start(bf16[896,512]{1,0:T(8,128)(2,1)} %param.15) | copy-start | bytes 2752516
  219.5 3.0 %copy-start.1 = (bf16[896,512]{1,0:T(8,128)(2,1)S(1)}, bf16[896,512]{1,0:T(8,128)(2,1)}, u32[]{:S(2)}) copy-start(bf16[896,512]{1,0:T(8,128)(2,1)} %param.14) | copy-start | bytes 2752516
Sparse Core Ops, SparseCore 0:
  17.4 64.0 reduce-scatter.1
  83.3 54.8 all-gather.3
  139.9 65.6 all-gather.5
where the time goes:
time: 229 us
  waiting for transfers between devices  128 us (56%)
  matrix products  33.5 us (15%)
  starting transfers between devices  27 us (12%)
  other arithmetic  16 us (7%)
  between operations  13.6 us (6%)
  local copies, waits for them, and re-layouts  10.6 us (5%)
    all_gather x1, waiting for transfers between devices, shards(): encoded = lax.all_gather(mine, 'tensor', axis=1, tiled=True)  52.7 us
    all_to_all x1, waiting for transfers between devices, shards(): lax.all_to_all(encoded_own[asked], 'dp', split_axis=0, concat_axis=0, til...  25.2 us
    reduce_scatter x1, waiting for transfers between devices, shards(): lax.psum_scatter(partial.astype(jnp.bfloat16), 'tensor', scatter_dimensio...  23.8 us
    ppermute x4, waiting for transfers between devices, ring_hops(): going_right = lax.ppermute(going_right, 'tensor', to_right)  17.8 us
    ppermute x3, starting transfers between devices, ring_hops(): going_left = lax.ppermute(going_left, 'tensor', to_left)  10.2 us
    ppermute x3, waiting for transfers between devices, ring_hops(): going_left = lax.ppermute(going_left, 'tensor', to_left)  7.73 us
    dot_general x1, matrix products, shards(): jnp.einsum('btf,fe->bte', active, w_down, preferred_element_type=jnp.floa...  7.69 us
    all_to_all x1, starting transfers between devices, shards(): lax.all_to_all(requests, 'dp', split_axis=0, concat_axis=0, tiled=True)  7.59 us
  transfers between devices with their start and end apart: 12, of which 10 were waited for; matrix products, arithmetic and copies ran while one was open for 13% of the time, Pallas kernels for 0%

commit v1 on v0

--- a/solution.py
+++ b/solution.py
@@ -121,7 +121,23 @@
     asked = lax.all_to_all(requests, "dp", split_axis=0, concat_axis=0, tiled=True)
     replies = lax.all_to_all(encoded_own[asked], "dp", split_axis=0, concat_axis=0, tiled=True)
     mine = replies.reshape(dp_count * capacity, rows_here, enc_width)[slots]
-    encoded = lax.all_gather(mine, "tensor", axis=1, tiled=True)
+    devices, index, span = (lax.axis_size("tensor"), lax.axis_index("tensor"), mine.shape[1])
+    right = [(i_2, (i_2 + 1) % devices) for i_2 in range(devices)]
+    left = [(i_2, (i_2 - 1) % devices) for i_2 in range(devices)]
+    encoded = jnp.zeros((*mine.shape[:1], devices * span, *mine.shape[1 + 1 :]), mine.dtype)
+    encoded = lax.dynamic_update_slice_in_dim(encoded, mine, index * span, axis=1)
+    from_left = from_right = mine
+    half = devices // 2
+    for k in range(1, half + 1):
+        from_left = lax.ppermute(from_left, "tensor", right)
+        encoded = lax.dynamic_update_slice_in_dim(
+            encoded, from_left, (index - k) % devices * span, axis=1
+        )
+        if k < devices - half:
+            from_right = lax.ppermute(from_right, "tensor", left)
+            encoded = lax.dynamic_update_slice_in_dim(
+                encoded, from_right, (index + k) % devices * span, axis=1
+            )
     heads_here = w_query.shape[1] // HD
     states_rest = lax.all_gather(states_rest, "tensor", axis=1, tiled=True)
     projected = jnp.concatenate(

time: 229 us -> 251 us (1.096); the launches traced: 229 us -> 248 us
  starting transfers between devices: 27 us -> 40.6 us
  waiting for transfers between devices: 128 us -> 131 us
    ppermute x0 -> x7, waiting for transfers between devices: none -> 76.2 us  [the longest x4 76.2 us: shards(): from_left = lax.ppermute(from_left, 'tensor', right)]
    all_gather x1 -> x0, waiting for transfers between devices: 52.7 us -> none  [shards(): encoded = lax.all_gather(mine, 'tensor', axis=1, tiled=True)]
    reduce_scatter x1, waiting for transfers between devices: 23.8 us -> 9.44 us  [shards(): lax.psum_scatter(partial.astype(jnp.bfloat16), 'tensor', scatter_dimensio...]
    ppermute x0 -> x7, starting transfers between devices: none -> 8.26 us  [the longest x3 7.99 us: shards(): from_right = lax.ppermute(from_right, 'tensor', left)]
    ppermute x4, waiting for transfers between devices: 17.8 us -> 11.4 us  [ring_hops(): going_right = lax.ppermute(going_right, 'tensor', to_right)]
    all_to_all x1, starting transfers between devices: 7.59 us -> 12.4 us  [shards(): lax.all_to_all(requests, 'dp', split_axis=0, concat_axis=0, tiled=True)]
  transfers between devices with their start and end apart: 12 -> 18, of which waited for: 10 -> 11; matrix products, arithmetic and copies ran while one was open for 13% -> 12% of each run, Pallas kernels for 0% -> 0%
where the time goes in v1:
time: 251 us; the launch traced here: 248 us
  waiting for transfers between devices  131 us (52%)
  starting transfers between devices  40.6 us (16%)
  matrix products  32.5 us (13%)
  other arithmetic  17.4 us (7%)
  between operations  14.2 us (6%)
  local copies, waits for them, and re-layouts  12.8 us (5%)
    ppermute x4, waiting for transfers between devices, shards(): from_left = lax.ppermute(from_left, 'tensor', right)  76.2 us
    all_to_all x1, waiting for transfers between devices, shards(): lax.all_to_all(encoded_own[asked], 'dp', split_axis=0, concat_axis=0, til...  24.7 us
    all_to_all x1, starting transfers between devices, shards(): lax.all_to_all(requests, 'dp', split_axis=0, concat_axis=0, tiled=True)  12.4 us
    ppermute x4, waiting for transfers between devices, ring_hops(): going_right = lax.ppermute(going_right, 'tensor', to_right)  11.4 us
    ppermute x3, starting transfers between devices, ring_hops(): going_left = lax.ppermute(going_left, 'tensor', to_left)  9.77 us
    reduce_scatter x1, waiting for transfers between devices, shards(): lax.psum_scatter(partial.astype(jnp.bfloat16), 'tensor', scatter_dimensio...  9.44 us
    ppermute x3, waiting for transfers between devices, ring_hops(): going_left = lax.ppermute(going_left, 'tensor', to_left)  8.2 us
    ppermute x3, starting transfers between devices, shards(): from_right = lax.ppermute(from_right, 'tensor', left)  7.99 us
  transfers between devices with their start and end apart: 18, of which 11 were waited for; matrix products, arithmetic and copies ran while one was open for 12% of the time, Pallas kernels for 0%

profile of v1, /device:TPU:1, one launch (start us, length us, event | category | flops | bytes accessed | tf_op | source)
XLA Modules:
  0.0 248.4 jit_solution(14088362952791232873)
XLA Ops:
  6.5 3.0 %multiply_reduce_fusion = f32[16,128]{1,0:T(8,128)S(1)} fusion(bf16[16,128,896]{2,1,0:T(8,128)(2,1)} %param.10), kind=kLoop, calls=%fused_computation.3 | loop fusion | flops 5502976 | bytes 3678208 | tf_op jit(solution)/shard_map/reduce_sum | solution.py:101
  9.6 7.7 %convolution_convert_fusion.1 = bf16[16,128,896]{2,1,0:T(8,128)(2,1)} fusion(f32[16,128]{1,0:T(8,128)S(1)} %add_rsqrt_fusion.2, bf16[16,128,896]{2,1,0:T(8,128)(2,1)} %param.10, bf16[448,896]{1,0:T(8,128)(2,1)S(1)} %copy-done.19, bf16[896,448]{0,1:T(8,128)(2,1)S(1)} %copy-done.20), kind=kOutput, calls=%fused_computation.26 | convolution fusion | flops 3303931904 | bytes 8953856 | tf_op jit(solution)/shard_map/btf,fe->bte/dot_general | solution.py:105
  18.4 2.5 %collective-permute-start.3 = (bf16[192,512]{1,0:T(8,128)(2,1)S(1)}, bf16[192,512]{1,0:T(8,128)(2,1)S(1)}, u32[]{:S(2)}, u32[]{:S(2)}) collective-permute-start(bf16[192,512]{1,0:T(8,128)(2,1)S(1)} %slice.14), channel_id=1, source_target_pairs={{0,1},{1,2},{2,3},{3,4},{4,5},{5,6},{6,7},{7,0},{8,9},{9,10},{10,1... | collective-permute-start | bytes 589832 | tf_op jit(solution)/shard_map/ppermute | solution.py:58
  21.0 4.0 %collective-permute-start = (bf16[192,512]{1,0:T(8,128)(2,1)S(1)}, bf16[192,512]{1,0:T(8,128)(2,1)S(1)}, u32[]{:S(2)}, u32[]{:S(2)}) collective-permute-start(bf16[192,512]{1,0:T(8,128)(2,1)S(1)} %slice.14), channel_id=1, source_target_pairs={{0,7},{1,0},{2,1},{3,2},{4,3},{5,4},{6,5},{7,6},{8,15},{9,8},{10,9... | collective-permute-start | bytes 589832 | tf_op jit(solution)/shard_map/ppermute | solution.py:61
  25.2 4.3 %collective-permute-done.3 = bf16[192,512]{1,0:T(8,128)(2,1)S(1)} collective-permute-done((bf16[192,512]{1,0:T(8,128)(2,1)S(1)}, bf16[192,512]{1,0:T(8,128)(2,1)S(1)}, u32[]{:S(2)}, u32[]{:S(2)}) %collective-permute-start.3) | collective-permute-done | bytes 196640 | tf_op jit(solution)/shard_map/ppermute | solution.py:58
  29.9 2.7 %collective-permute-start.1 = (bf16[192,512]{1,0:T(8,128)(2,1)S(1)}, bf16[192,512]{1,0:T(8,128)(2,1)S(1)}, u32[]{:S(2)}, u32[]{:S(2)}) collective-permute-start(bf16[192,512]{1,0:T(8,128)(2,1)S(1)} %collective-permute-done), channel_id=1, source_target_pairs={{0,7},{1,0},{2,1},{3,2},{4,3},{5,4},{6,5},{7,6},{8,15},{9,8},{10,9... | collective-permute-start | bytes 589832 | tf_op jit(solution)/shard_map/ppermute | solution.py:61
  32.6 3.3 %collective-permute-done.4 = bf16[192,512]{1,0:T(8,128)(2,1)S(1)} collective-permute-done((bf16[192,512]{1,0:T(8,128)(2,1)S(1)}, bf16[192,512]{1,0:T(8,128)(2,1)S(1)}, u32[]{:S(2)}, u32[]{:S(2)}) %collective-permute-start.4) | collective-permute-done | bytes 196640 | tf_op jit(solution)/shard_map/ppermute | solution.py:58
  36.8 12.4 %all-to-all-start = ((s32[32,1,2]{2,1,0:T(1,128)}), s32[32,1,2]{2,1,0:T(1,128)S(1)}, u32[]{:S(2)}, u32[]{:S(2)}) async-start(s32[32,1,2]{2,1,0:T(1,128)} %bitcast.2), calls=%async_computation.1 | async-start | bytes 32768 | tf_op jit(solution)/shard_map/all_to_all | solution.py:121
  50.1 5.8 %convert_element_type.41 = f32[16,128,896]{2,1,0:T(8,128)} convert(bf16[16,128,896]{2,1,0:T(8,128)(2,1)} %param.10) | non-fusion elementwise | flops 1835008 | bytes 11010048 | tf_op jit(solution)/shard_map/convert_element_type | solution.py:99
  56.2 3.0 %collective-permute-start.2 = (bf16[192,512]{1,0:T(8,128)(2,1)S(1)}, bf16[192,512]{1,0:T(8,128)(2,1)S(1)}, u32[]{:S(2)}, u32[]{:S(2)}) collective-permute-start(bf16[192,512]{1,0:T(8,128)(2,1)S(1)} %collective-permute-done.1), channel_id=1, source_target_pairs={{0,7},{1,0},{2,1},{3,2},{4,3},{5,4},{6,5},{7,6},{8,15},{9,8},{10,9... | collective-permute-start | bytes 589832 | tf_op jit(solution)/shard_map/ppermute | solution.py:61
  59.4 8.2 %collective-permute-done.2 = bf16[192,512]{1,0:T(8,128)(2,1)S(1)} collective-permute-done((bf16[192,512]{1,0:T(8,128)(2,1)S(1)}, bf16[192,512]{1,0:T(8,128)(2,1)S(1)}, u32[]{:S(2)}, u32[]{:S(2)}) %collective-permute-start.2) | collective-permute-done | bytes 196640 | tf_op jit(solution)/shard_map/ppermute | solution.py:61
  67.6 3.7 %collective-permute-done.6 = bf16[192,512]{1,0:T(8,128)(2,1)S(1)} collective-permute-done((bf16[192,512]{1,0:T(8,128)(2,1)S(1)}, bf16[192,512]{1,0:T(8,128)(2,1)S(1)}, u32[]{:S(2)}, u32[]{:S(2)}) %collective-permute-start.6) | collective-permute-done | bytes 196640 | tf_op jit(solution)/shard_map/ppermute | solution.py:58
  72.0 9.4 %reduce-scatter.2.cloned.1.call-done = bf16[16,16,896]{2,1,0:T(8,128)(2,1)} async-done(((bf16[16,128,896]{2,1,0:T(8,128)(2,1)}), bf16[16,16,896]{2,1,0:T(8,128)(2,1)}) %reduce-scatter.2.cloned.1.call-update) | async-done | bytes 458768 | tf_op jit(solution)/shard_map/reduce_scatter | solution.py:112
  82.9 2.0 gather_fusion
  84.9 7.6 %all-to-all-start.1 = ((bf16[32,2,16,896]{3,2,1,0:T(8,128)(2,1)}), bf16[32,2,16,896]{3,2,1,0:T(8,128)(2,1)S(1)}, u32[]{:S(2)}, u32[]{:S(2)}) async-start(bf16[32,2,16,896]{3,2,1,0:T(8,128)(2,1)} %bitcast.4), calls=%async_computation.2 | async-start | bytes 3670016 | tf_op jit(solution)/shard_map/all_to_all | solution.py:122
  93.4 24.7 %all-to-all-done.1 = bf16[32,2,16,896]{3,2,1,0:T(8,128)(2,1)S(1)} async-done(((bf16[32,2,16,896]{3,2,1,0:T(8,128)(2,1)}), bf16[32,2,16,896]{3,2,1,0:T(8,128)(2,1)S(1)}, u32[]{:S(2)}, u32[]{:S(2)}) %all-to-all-start.1) | async-done | bytes 1835040 | tf_op jit(solution)/shard_map/all_to_all | solution.py:122
  119.3 1.6 fusion.60
  120.8 1.4 fusion.58
  122.3 2.5 %collective-permute-start.8 = (bf16[24,16,896]{2,1,0:T(8,128)(2,1)S(1)}, bf16[24,16,896]{2,1,0:T(8,128)(2,1)S(1)}, u32[]{:S(2)}, u32[]{:S(2)}) collective-permute-start(bf16[24,16,896]{2,1,0:T(8,128)(2,1)S(1)} %gather_fusion.1), channel_id=1, source_target_pairs={{0,7},{1,0},{2,1},{3,2},{4,3},{5,4},{6,5},{7,6},{8,15},{9,8},{10,9... | collective-permute-start | bytes 2064392 | tf_op jit(solution)/shard_map/ppermute | solution.py:137
  124.8 27.5 %collective-permute-done.7 = bf16[24,16,896]{2,1,0:T(8,128)(2,1)S(1)} collective-permute-done((bf16[24,16,896]{2,1,0:T(8,128)(2,1)S(1)}, bf16[24,16,896]{2,1,0:T(8,128)(2,1)S(1)}, u32[]{:S(2)}, u32[]{:S(2)}) %collective-permute-start.7) | collective-permute-done | bytes 688160 | tf_op jit(solution)/shard_map/ppermute | solution.py:132
  153.7 1.4 fusion.54
  155.5 2.8 %collective-permute-start.10 = (bf16[24,16,896]{2,1,0:T(8,128)(2,1)S(1)}, bf16[24,16,896]{2,1,0:T(8,128)(2,1)S(1)}, u32[]{:S(2)}, u32[]{:S(2)}) collective-permute-start(bf16[24,16,896]{2,1,0:T(8,128)(2,1)S(1)} %collective-permute-done.8), channel_id=1, source_target_pairs={{0,7},{1,0},{2,1},{3,2},{4,3},{5,4},{6,5},{7,6},{8,15},{9,8},{10,9... | collective-permute-start | bytes 2064392 | tf_op jit(solution)/shard_map/ppermute | solution.py:137
  158.2 20.4 %collective-permute-done.9 = bf16[24,16,896]{2,1,0:T(8,128)(2,1)S(1)} collective-permute-done((bf16[24,16,896]{2,1,0:T(8,128)(2,1)S(1)}, bf16[24,16,896]{2,1,0:T(8,128)(2,1)S(1)}, u32[]{:S(2)}, u32[]{:S(2)}) %collective-permute-start.9) | collective-permute-done | bytes 688160 | tf_op jit(solution)/shard_map/ppermute | solution.py:132
  179.5 2.7 %collective-permute-start.12 = (bf16[24,16,896]{2,1,0:T(8,128)(2,1)S(1)}, bf16[24,16,896]{2,1,0:T(8,128)(2,1)S(1)}, u32[]{:S(2)}, u32[]{:S(2)}) collective-permute-start(bf16[24,16,896]{2,1,0:T(8,128)(2,1)S(1)} %collective-permute-done.10), channel_id=1, source_target_pairs={{0,7},{1,0},{2,1},{3,2},{4,3},{5,4},{6,5},{7,6},{8,15},{9,8},{10,9... | collective-permute-start | bytes 2064392 | tf_op jit(solution)/shard_map/ppermute | solution.py:137
  183.2 12.7 %collective-permute-done.11 = bf16[24,16,896]{2,1,0:T(8,128)(2,1)S(1)} collective-permute-done((bf16[24,16,896]{2,1,0:T(8,128)(2,1)S(1)}, bf16[24,16,896]{2,1,0:T(8,128)(2,1)S(1)}, u32[]{:S(2)}, u32[]{:S(2)}) %collective-permute-start.11) | collective-permute-done | bytes 688160 | tf_op jit(solution)/shard_map/ppermute | solution.py:132
  196.6 15.6 %collective-permute-done.13 = bf16[24,16,896]{2,1,0:T(8,128)(2,1)S(1)} collective-permute-done((bf16[24,16,896]{2,1,0:T(8,128)(2,1)S(1)}, bf16[24,16,896]{2,1,0:T(8,128)(2,1)S(1)}, u32[]{:S(2)}, u32[]{:S(2)}) %collective-permute-start.13) | collective-permute-done | bytes 688160 | tf_op jit(solution)/shard_map/ppermute | solution.py:132
  212.4 4.4 %fusion = (f32[4,3072]{1,0:T(4,128)S(1)}, f32[3072,4,128]{2,0,1:T(8,128)S(1)}) fusion(bf16[3072,896,1]{1,0,2:T(8,128)(2,1)S(1)} %bitcast.75, bf16[896,512]{1,0:T(8,128)(2,1)S(1)} %copy-done), kind=kOutput, calls=%fused_computation.6 | convolution fusion | flops 2821705728 | bytes 12763136 | tf_op jit(solution)/shard_map/ke,ehd->hkd/dot_general | solution.py:154
  216.8 5.0 %convolution_convert_fusion = bf16[3072,4,128]{2,0,1:T(8,128)(2,1)} fusion(bf16[3072,896,1]{1,0,2:T(8,128)(2,1)S(1)} %bitcast.76, bf16[896,512]{1,0:T(8,128)(2,1)S(1)} %copy-done.18), kind=kOutput, calls=%fused_computation.9 | convolution fusion | flops 2820145152 | bytes 9568256 | tf_op jit(solution)/shard_map/ke,ehd->hkd/dot_general | solution.py:161
  221.8 3.3 %fusion.1 = bf16[4,3072,128]{2,1,0:T(8,128)(2,1)} fusion(f32[3072,4,128]{2,0,1:T(8,128)S(1)} %get-tuple-element.28, f32[4,3072]{1,0:T(4,128)S(1)} %add_rsqrt_fusion.1), kind=kLoop, calls=%fused_computation.7 | loop fusion | flops 3145728 | bytes 9486336 | tf_op jit(solution)/shard_map/convert_element_type | solution.py:45
  225.1 5.8 %fusion.77 = f32[513,512]{1,0:T(8,128)S(1)} fusion(bf16[513,4096]{1,0:T(8,128)(2,1)} %all-gather.2.cloned.1.call-done, bf16[4096,512]{1,0:T(8,128)(2,1)} %param.13), kind=kOutput, calls=%fused_computation.115 | convolution fusion | flops 2151677952 | bytes 9447424 | tf_op jit(solution)/shard_map/dot_general | solution.py:146
  232.2 1.7 reshape.246
  234.8 1.7 fusion.47
  (109 shorter events, 19.2 us)
Async XLA Ops:
  6.5 205.8 %copy-start = (bf16[896,512]{1,0:T(8,128)(2,1)S(1)}, bf16[896,512]{1,0:T(8,128)(2,1)}, u32[]{:S(2)}) copy-start(bf16[896,512]{1,0:T(8,128)(2,1)} %param.14) | copy-start | bytes 2752516
  6.5 74.9 %reduce-scatter.2.cloned.1.call-start = ((), (), s32[]{:S(2)}) async-start(), calls=%async_computation.3 | async-start | bytes 4128768 | tf_op jit(solution)/shard_map/reduce_scatter | solution.py:112
  17.3 7.8 %copy-start.17 = (s32[12,2]{0,1:T(2,128)S(1)}, s32[12,2]{0,1:T(2,128)}, u32[]{:S(2)}) copy-start(s32[12,2]{0,1:T(2,128)} %param.9) | copy-start | bytes 292
  18.4 37.5 %copy-start.4 = (bf16[192,512]{1,0:T(8,128)(2,1)}, bf16[192,512]{1,0:T(8,128)(2,1)S(1)}, u32[]{:S(2)}) copy-start(bf16[192,512]{1,0:T(8,128)(2,1)S(1)} %slice.14) | copy-start | bytes 589828
  18.4 11.1 %collective-permute-start.3 = (bf16[192,512]{1,0:T(8,128)(2,1)S(1)}, bf16[192,512]{1,0:T(8,128)(2,1)S(1)}, u32[]{:S(2)}, u32[]{:S(2)}) collective-permute-start(bf16[192,512]{1,0:T(8,128)(2,1)S(1)} %slice.14), channel_id=1, source_target_pairs={{0,1},{1,2},{2,3},{3,4},{4,5},{5,6},{6,7},{7,0},{8,9},{9,10},{10,1... | collective-permute-start | bytes 589832 | tf_op jit(solution)/shard_map/ppermute | solution.py:58
  21.0 8.9 %collective-permute-start = (bf16[192,512]{1,0:T(8,128)(2,1)S(1)}, bf16[192,512]{1,0:T(8,128)(2,1)S(1)}, u32[]{:S(2)}, u32[]{:S(2)}) collective-permute-start(bf16[192,512]{1,0:T(8,128)(2,1)S(1)} %slice.14), channel_id=1, source_target_pairs={{0,7},{1,0},{2,1},{3,2},{4,3},{5,4},{6,5},{7,6},{8,15},{9,8},{10,9... | collective-permute-start | bytes 589832 | tf_op jit(solution)/shard_map/ppermute | solution.py:61
  29.5 26.4 %copy-start.7 = (bf16[192,512]{1,0:T(8,128)(2,1)}, bf16[192,512]{1,0:T(8,128)(2,1)S(1)}, u32[]{:S(2)}) copy-start(bf16[192,512]{1,0:T(8,128)(2,1)S(1)} %collective-permute-done.3) | copy-start | bytes 589828
  29.5 6.4 %collective-permute-start.4 = (bf16[192,512]{1,0:T(8,128)(2,1)S(1)}, bf16[192,512]{1,0:T(8,128)(2,1)S(1)}, u32[]{:S(2)}, u32[]{:S(2)}) collective-permute-start(bf16[192,512]{1,0:T(8,128)(2,1)S(1)} %collective-permute-done.3), channel_id=1, source_target_pairs={{0,1},{1,2},{2,3},{3,4},{4,5},{5,6},{6,7},{7,0},{8,9},{9,10},{10,1... | collective-permute-start | bytes 589832 | tf_op jit(solution)/shard_map/ppermute | solution.py:58
  29.8 26.1 %copy-start.11 = (bf16[192,512]{1,0:T(8,128)(2,1)}, bf16[192,512]{1,0:T(8,128)(2,1)S(1)}, u32[]{:S(2)}) copy-start(bf16[192,512]{1,0:T(8,128)(2,1)S(1)} %collective-permute-done) | copy-start | bytes 589828
  29.9 26.4 %collective-permute-start.1 = (bf16[192,512]{1,0:T(8,128)(2,1)S(1)}, bf16[192,512]{1,0:T(8,128)(2,1)S(1)}, u32[]{:S(2)}, u32[]{:S(2)}) collective-permute-start(bf16[192,512]{1,0:T(8,128)(2,1)S(1)} %collective-permute-done), channel_id=1, source_target_pairs={{0,7},{1,0},{2,1},{3,2},{4,3},{5,4},{6,5},{7,6},{8,15},{9,8},{10,9... | collective-permute-start | bytes 589832 | tf_op jit(solution)/shard_map/ppermute | solution.py:61
  35.9 20.0 %copy-start.9 = (bf16[192,512]{1,0:T(8,128)(2,1)}, bf16[192,512]{1,0:T(8,128)(2,1)S(1)}, u32[]{:S(2)}) copy-start(bf16[192,512]{1,0:T(8,128)(2,1)S(1)} %collective-permute-done.4) | copy-start | bytes 589828
  35.9 23.3 %collective-permute-start.5 = (bf16[192,512]{1,0:T(8,128)(2,1)S(1)}, bf16[192,512]{1,0:T(8,128)(2,1)S(1)}, u32[]{:S(2)}, u32[]{:S(2)}) collective-permute-start(bf16[192,512]{1,0:T(8,128)(2,1)S(1)} %collective-permute-done.4), channel_id=1, source_target_pairs={{0,1},{1,2},{2,3},{3,4},{4,5},{5,6},{6,7},{7,0},{8,9},{9,10},{10,1... | collective-permute-start | bytes 589832 | tf_op jit(solution)/shard_map/ppermute | solution.py:58
  36.8 19.4 %all-to-all-start = ((s32[32,1,2]{2,1,0:T(1,128)}), s32[32,1,2]{2,1,0:T(1,128)S(1)}, u32[]{:S(2)}, u32[]{:S(2)}) async-start(s32[32,1,2]{2,1,0:T(1,128)} %bitcast.2), calls=%async_computation.1 | async-start | bytes 32768 | tf_op jit(solution)/shard_map/all_to_all | solution.py:121
  56.2 28.7 %copy-start.14 = (bf16[192,512]{1,0:T(8,128)(2,1)}, bf16[192,512]{1,0:T(8,128)(2,1)S(1)}, u32[]{:S(2)}) copy-start(bf16[192,512]{1,0:T(8,128)(2,1)S(1)} %collective-permute-done.1) | copy-start | bytes 589828
  56.2 11.4 %collective-permute-start.2 = (bf16[192,512]{1,0:T(8,128)(2,1)S(1)}, bf16[192,512]{1,0:T(8,128)(2,1)S(1)}, u32[]{:S(2)}, u32[]{:S(2)}) collective-permute-start(bf16[192,512]{1,0:T(8,128)(2,1)S(1)} %collective-permute-done.1), channel_id=1, source_target_pairs={{0,7},{1,0},{2,1},{3,2},{4,3},{5,4},{6,5},{7,6},{8,15},{9,8},{10,9... | collective-permute-start | bytes 589832 | tf_op jit(solution)/shard_map/ppermute | solution.py:61
  59.2 25.7 %copy-start.12 = (bf16[192,512]{1,0:T(8,128)(2,1)}, bf16[192,512]{1,0:T(8,128)(2,1)S(1)}, u32[]{:S(2)}) copy-start(bf16[192,512]{1,0:T(8,128)(2,1)S(1)} %collective-permute-done.5) | copy-start | bytes 589828
  59.2 12.2 %collective-permute-start.6 = (bf16[192,512]{1,0:T(8,128)(2,1)S(1)}, bf16[192,512]{1,0:T(8,128)(2,1)S(1)}, u32[]{:S(2)}, u32[]{:S(2)}) collective-permute-start(bf16[192,512]{1,0:T(8,128)(2,1)S(1)} %collective-permute-done.5), channel_id=1, source_target_pairs={{0,1},{1,2},{2,3},{3,4},{4,5},{5,6},{6,7},{7,0},{8,9},{9,10},{10,1... | collective-permute-start | bytes 589832 | tf_op jit(solution)/shard_map/ppermute | solution.py:58
  67.6 17.3 %copy-start.15 = (bf16[192,512]{1,0:T(8,128)(2,1)}, bf16[192,512]{1,0:T(8,128)(2,1)S(1)}, u32[]{:S(2)}) copy-start(bf16[192,512]{1,0:T(8,128)(2,1)S(1)} %collective-permute-done.2) | copy-start | bytes 589828
  84.9 33.1 %all-to-all-start.1 = ((bf16[32,2,16,896]{3,2,1,0:T(8,128)(2,1)}), bf16[32,2,16,896]{3,2,1,0:T(8,128)(2,1)S(1)}, u32[]{:S(2)}, u32[]{:S(2)}) async-start(bf16[32,2,16,896]{3,2,1,0:T(8,128)(2,1)} %bitcast.4), calls=%async_computation.2 | async-start | bytes 3670016 | tf_op jit(solution)/shard_map/all_to_all | solution.py:122
  92.5 132.5 %all-gather.2.cloned.1.call-start = ((), (), s32[]{:S(2)}) async-start(), calls=%async_computation.4 | async-start | bytes 4792320 | tf_op jit(solution)/shard_map/all_gather | solution.py:142
  118.7 36.4 %copy-start.13 = (bf16[192,512]{1,0:T(8,128)(2,1)S(1)}, bf16[192,512]{1,0:T(8,128)(2,1)}, u32[]{:S(2)}) copy-start(bf16[192,512]{1,0:T(8,128)(2,1)} %copy-done.12) | copy-start | bytes 589828
  118.7 59.9 %copy-start.10 = (bf16[192,512]{1,0:T(8,128)(2,1)S(1)}, bf16[192,512]{1,0:T(8,128)(2,1)}, u32[]{:S(2)}) copy-start(bf16[192,512]{1,0:T(8,128)(2,1)} %copy-done.9) | copy-start | bytes 589828
  118.8 60.1 %copy-start.8 = (bf16[192,512]{1,0:T(8,128)(2,1)S(1)}, bf16[192,512]{1,0:T(8,128)(2,1)}, u32[]{:S(2)}) copy-start(bf16[192,512]{1,0:T(8,128)(2,1)} %copy-done.7) | copy-start | bytes 589828
  118.8 33.5 %collective-permute-start.7 = (bf16[24,16,896]{2,1,0:T(8,128)(2,1)S(1)}, bf16[24,16,896]{2,1,0:T(8,128)(2,1)S(1)}, u32[]{:S(2)}, u32[]{:S(2)}) collective-permute-start(bf16[24,16,896]{2,1,0:T(8,128)(2,1)S(1)} %gather_fusion.1), channel_id=1, source_target_pairs={{0,1},{1,2},{2,3},{3,4},{4,5},{5,6},{6,7},{7,0},{8,9},{9,10},{10,1... | collective-permute-start | bytes 2064392 | tf_op jit(solution)/shard_map/ppermute | solution.py:132
  119.3 35.9 %copy-start.3 = (bf16[4096,512]{1,0:T(8,128)(2,1)S(1)}, bf16[4096,512]{1,0:T(8,128)(2,1)}, u32[]{:S(2)}) copy-start(bf16[4096,512]{1,0:T(8,128)(2,1)} %param.13) | copy-start | bytes 12582916
  119.3 59.9 %copy-start.5 = (bf16[192,512]{1,0:T(8,128)(2,1)S(1)}, bf16[192,512]{1,0:T(8,128)(2,1)}, u32[]{:S(2)}) copy-start(bf16[192,512]{1,0:T(8,128)(2,1)} %copy-done.4) | copy-start | bytes 589828
  122.3 33.2 %collective-permute-start.8 = (bf16[24,16,896]{2,1,0:T(8,128)(2,1)S(1)}, bf16[24,16,896]{2,1,0:T(8,128)(2,1)S(1)}, u32[]{:S(2)}, u32[]{:S(2)}) collective-permute-start(bf16[24,16,896]{2,1,0:T(8,128)(2,1)S(1)} %gather_fusion.1), channel_id=1, source_target_pairs={{0,7},{1,0},{2,1},{3,2},{4,3},{5,4},{6,5},{7,6},{8,15},{9,8},{10,9... | collective-permute-start | bytes 2064392 | tf_op jit(solution)/shard_map/ppermute | solution.py:137
  152.3 26.3 %collective-permute-start.9 = (bf16[24,16,896]{2,1,0:T(8,128)(2,1)S(1)}, bf16[24,16,896]{2,1,0:T(8,128)(2,1)S(1)}, u32[]{:S(2)}, u32[]{:S(2)}) collective-permute-start(bf16[24,16,896]{2,1,0:T(8,128)(2,1)S(1)} %collective-permute-done.7), channel_id=1, source_target_pairs={{0,1},{1,2},{2,3},{3,4},{4,5},{5,6},{6,7},{7,0},{8,9},{9,10},{10,1... | collective-permute-start | bytes 2064392 | tf_op jit(solution)/shard_map/ppermute | solution.py:132
  155.5 24.1 %collective-permute-start.10 = (bf16[24,16,896]{2,1,0:T(8,128)(2,1)S(1)}, bf16[24,16,896]{2,1,0:T(8,128)(2,1)S(1)}, u32[]{:S(2)}, u32[]{:S(2)}) collective-permute-start(bf16[24,16,896]{2,1,0:T(8,128)(2,1)S(1)} %collective-permute-done.8), channel_id=1, source_target_pairs={{0,7},{1,0},{2,1},{3,2},{4,3},{5,4},{6,5},{7,6},{8,15},{9,8},{10,9... | collective-permute-start | bytes 2064392 | tf_op jit(solution)/shard_map/ppermute | solution.py:137
  178.6 17.2 %collective-permute-start.11 = (bf16[24,16,896]{2,1,0:T(8,128)(2,1)S(1)}, bf16[24,16,896]{2,1,0:T(8,128)(2,1)S(1)}, u32[]{:S(2)}, u32[]{:S(2)}) collective-permute-start(bf16[24,16,896]{2,1,0:T(8,128)(2,1)S(1)} %collective-permute-done.9), channel_id=1, source_target_pairs={{0,1},{1,2},{2,3},{3,4},{4,5},{5,6},{6,7},{7,0},{8,9},{9,10},{10,1... | collective-permute-start | bytes 2064392 | tf_op jit(solution)/shard_map/ppermute | solution.py:132
  179.5 17.0 %collective-permute-start.12 = (bf16[24,16,896]{2,1,0:T(8,128)(2,1)S(1)}, bf16[24,16,896]{2,1,0:T(8,128)(2,1)S(1)}, u32[]{:S(2)}, u32[]{:S(2)}) collective-permute-start(bf16[24,16,896]{2,1,0:T(8,128)(2,1)S(1)} %collective-permute-done.10), channel_id=1, source_target_pairs={{0,7},{1,0},{2,1},{3,2},{4,3},{5,4},{6,5},{7,6},{8,15},{9,8},{10,9... | collective-permute-start | bytes 2064392 | tf_op jit(solution)/shard_map/ppermute | solution.py:137
  195.9 16.4 %collective-permute-start.13 = (bf16[24,16,896]{2,1,0:T(8,128)(2,1)S(1)}, bf16[24,16,896]{2,1,0:T(8,128)(2,1)S(1)}, u32[]{:S(2)}, u32[]{:S(2)}) collective-permute-start(bf16[24,16,896]{2,1,0:T(8,128)(2,1)S(1)} %collective-permute-done.11), channel_id=1, source_target_pairs={{0,1},{1,2},{2,3},{3,4},{4,5},{5,6},{6,7},{7,0},{8,9},{9,10},{10,1... | collective-permute-start | bytes 2064392 | tf_op jit(solution)/shard_map/ppermute | solution.py:132
  (8 other events, 19.8 us)
Sparse Core Ops, SparseCore 0:
  17.4 64.0 reduce-scatter.1
  95.2 76.5 all-gather.1
